TPU v7x, 256 devices: a whole 4x4x8 slice. The times are simulated.
256 devices in a mesh: date: 64 (over x, y, z_lo, core), rng: 4 (over z_hi).
Axes of the slice: x: 4, y: 4, z: 8 (z_hi: 4, z_lo: 2; z = z_hi * 2 + z_lo), core: 2. Of those that a mesh axis runs over, the one named last changes fastest.
Arguments:
- slc_re: bfloat16 [64, 2048, 512], P('date', None, 'rng'), may hold values from -170 to 170
- slc_im: bfloat16 [64, 2048, 512], P('date', None, 'rng'), may hold values from -170 to 170
- ref_date: int32 [1], replicated, may hold values from 0 to 63
- gain: float32 [2048], replicated, may hold values from 0.25 to 2
- bperp: int32 [64], replicated, may hold values from -200 to 199
- tdays: int32 [64], replicated, may hold values from 0 to 1899
- mask: int32 [2048, 512], P(None, 'rng'), may hold values from 0 to 1, as said below
Outputs:
- periodogram: float32 [2048, 512, 256], P('date', 'rng')
Inputs may be any that keep to these rules, and one draw needn't show every extreme that they name: `mask`: each aligned block of 32 lines by 128 range columns holds exactly 1024 candidates.
All inputs are finite; a program needn't handle non-finite values.
Results may differ from a plain program's by a relative error of at most 0.0067.
Values may be sent and summed in bfloat16 or wider, within the bound.
No kernel may reach another device: no remote copies, remote signals or barrier semaphores. Data moves between devices by JAX's collectives and lax.ppermute only.
A program may use at most 64 MiB of HBM per device.

v0:
```python
import math
import jax
import jax.numpy as jnp
from jax import lax
from jax.sharding import PartitionSpec as P

HGRID = 16
VGRID = 16
PHASE_Q = 1024


def broadcast(shard, axis, root):
    mine = lax.axis_index(axis) == root
    return lax.psum(jnp.where(mine, shard, jnp.zeros_like(shard)), axis)


def dft_tables(length):
    positions = jnp.arange(length, dtype=jnp.int32)
    products = positions[:, None] * positions[None, :] % length
    angles = products.astype(jnp.float32) * (2.0 * math.pi / length)
    return (jnp.cos(angles).astype(jnp.bfloat16), jnp.sin(angles).astype(jnp.bfloat16))


def phase_tables(bperp, tdays):
    grid_points = jnp.arange(HGRID * VGRID, dtype=jnp.int32)
    height_step = grid_points // VGRID
    speed_step = grid_points % VGRID
    quanta = (
        bperp[:, None] * height_step[None, :] + tdays[:, None] * speed_step[None, :]
    ) % PHASE_Q
    angles = quanta.astype(jnp.float32) * (2.0 * math.pi / PHASE_Q)
    phase_re = jnp.cos(angles).astype(jnp.bfloat16)
    phase_im = jnp.sin(angles).astype(jnp.bfloat16)
    upper = jnp.concatenate([phase_re, -phase_im], axis=1)
    lower = jnp.concatenate([phase_im, phase_re], axis=1)
    return jnp.concatenate([upper, lower], axis=0)


def coherence_map(piece_re, piece_im, phase_table):
    date_count = piece_re.shape[0]
    grid_size = phase_table.shape[1] // 2
    stacked = jnp.concatenate([piece_re, piece_im], axis=0)
    spectra = lax.dot_general(
        stacked, phase_table, (((0,), (0,)), ((), ())), preferred_element_type=jnp.float32
    )
    peri_re = spectra[:, :grid_size]
    peri_im = spectra[:, grid_size:]
    wide_re = piece_re.astype(jnp.float32)
    wide_im = piece_im.astype(jnp.float32)
    pixel_power = jnp.sum(wide_re * wide_re + wide_im * wide_im, axis=0) / date_count
    return (peri_re * peri_re + peri_im * peri_im) / (date_count * jnp.maximum(pixel_power, 1.0))[
        :, None
    ]


def shards(slc_re, slc_im, ref_date, gain, bperp, tdays, mask):
    date_dev, lines, rg_dev = slc_re.shape
    date_axis = lax.axis_size("date")
    pixel_total = lines * rg_dev * lax.axis_size("rng")
    ref_index = ref_date[0]
    owner_index = ref_index // date_dev
    owner_slot = ref_index % date_dev
    own_re = lax.dynamic_index_in_dim(slc_re, owner_slot, 0, keepdims=False)
    own_im = lax.dynamic_index_in_dim(slc_im, owner_slot, 0, keepdims=False)
    ref_re, ref_im = (
        broadcast(own_re, "date", owner_index),
        broadcast(own_im, "date", owner_index),
    )
    wide_re = slc_re.astype(jnp.float32)
    wide_im = slc_im.astype(jnp.float32)
    ref_wide_re = ref_re.astype(jnp.float32)
    ref_wide_im = ref_im.astype(jnp.float32)
    local_sums = jnp.sum(wide_re * wide_re + wide_im * wide_im, axis=(1, 2))
    ref_local = jnp.sum(ref_wide_re * ref_wide_re + ref_wide_im * ref_wide_im)
    date_sums, ref_sum = lax.psum((local_sums, ref_local), "rng")
    scales = lax.rsqrt(date_sums / pixel_total + 1e-06)
    ref_scale = lax.rsqrt(ref_sum / pixel_total + 1e-06)
    own_part_re = wide_re * scales[:, None, None]
    own_part_im = wide_im * scales[:, None, None]
    ref_part_re = (ref_wide_re * ref_scale)[None]
    ref_part_im = (ref_wide_im * ref_scale)[None]
    ifg_re = (own_part_re * ref_part_re + own_part_im * ref_part_im).astype(jnp.bfloat16)
    ifg_im = (own_part_im * ref_part_re - own_part_re * ref_part_im).astype(jnp.bfloat16)
    cos_table, sin_table = dft_tables(lines)
    pair = jnp.stack([ifg_re, ifg_im])
    cos_part = jnp.einsum("fl,kdlc->kdfc", cos_table, pair, preferred_element_type=jnp.float32)
    sin_part = jnp.einsum("fl,kdlc->kdfc", sin_table, pair, preferred_element_type=jnp.float32)
    spec_re = cos_part[0] + sin_part[1]
    spec_im = cos_part[1] - sin_part[0]
    weights = gain[:, None]
    held = jnp.stack(
        [(spec_re * weights).astype(jnp.bfloat16), (spec_im * weights).astype(jnp.bfloat16)]
    )
    back_cos = jnp.einsum("fl,kdfc->kdlc", cos_table, held, preferred_element_type=jnp.float32)
    back_sin = jnp.einsum("fl,kdfc->kdlc", sin_table, held, preferred_element_type=jnp.float32)
    filt_re = ((back_cos[0] - back_sin[1]) * (1.0 / lines)).astype(jnp.bfloat16)
    filt_im = ((back_sin[0] + back_cos[1]) * (1.0 / lines)).astype(jnp.bfloat16)
    phase_table = phase_tables(bperp, tdays)
    grid_size = HGRID * VGRID
    lines_dev = lines // date_axis
    my_index = lax.axis_index("date")
    piece_re = lax.all_to_all(filt_re, "date", split_axis=1, concat_axis=0, tiled=True)
    piece_im = lax.all_to_all(filt_im, "date", split_axis=1, concat_axis=0, tiled=True)
    row_count = piece_re.shape[1]
    col_count = piece_re.shape[2]
    flat_re = piece_re.reshape(piece_re.shape[0], row_count * col_count)
    flat_im = piece_im.reshape(piece_im.shape[0], row_count * col_count)
    result = coherence_map(flat_re, flat_im, phase_table)
    mapped = result.reshape(row_count, col_count, grid_size)
    mask_rows = lax.dynamic_slice_in_dim(mask, my_index * lines_dev, lines_dev, 0)
    return mapped * mask_rows.astype(jnp.float32)[:, :, None]


def solution(mesh):
    in_specs = (P("date", None, "rng"), P("date", None, "rng"), P(), P(), P(), P(), P(None, "rng"))
    out_specs = P("date", "rng", None)
    return jax.shard_map(shards, mesh=mesh, in_specs=in_specs, out_specs=out_specs, check_vma=False)
```

profile of v0, /device:TPU:1, one launch (start us, length us, event | category | flops | bytes accessed | tf_op | source)
XLA Modules:
  0.0 924.3 jit_solution(13972574443800671142)
XLA Ops:
  6.5 0.0 all-reduce.4.cloned.1.call-start
  6.5 1.2 copy.20
  7.8 1.2 copy.21
  9.7 1.1 select_bitcast_fusion
  10.8 0.0 all-reduce.4.cloned.1.call-update
  10.8 0.9 fusion.39
  11.7 561.3 %all-reduce.4.cloned.1.call-done = (bf16[2048,128]{0,1:T(8,128)(2,1)}, bf16[2048,128]{0,1:T(8,128)(2,1)}) async-done(((bf16[2048,128]{0,1:T(8,128)(2,1)}, bf16[2048,128]{0,1:T(8,128)(2,1)}), (bf16[2048,128]{0,1:T(8,128)(2,1)}, bf16[2048,128]{0,1:T(8,128)(2,1)})) %all-reduce.4.cloned.1.call-update) | async-done | bytes 1048592 | tf_op jit(solution)/shard_map/psum | solution.py:14
  572.9 2.1 fusion.41
  575.0 10.5 %all-reduce = (f32[]{:T(128)}, f32[1]{0:T(128)}) all-reduce(f32[]{:T(128)} %fusion.41, f32[1]{0:T(128)} %bitcast), channel_id=1, replica_groups=mesh['date'=64,'rng'=4] {'rng'}, use_global_device_ids=true, to_apply=%region_5.6 | all-reduce | flops 2 | bytes 16 | tf_op jit(solution)/shard_map/psum | solution.py:75
  587.0 1.7 fusion.59
  588.7 0.1 maximum_bitcast_fusion.18
  588.8 0.1 maximum_bitcast_fusion.20
  588.9 63.5 %fusion.18 = f32[2,1,2048,128]{2,3,0,1:T(8,128)S(1)} fusion(bf16[2,2048,128]{1,2,0:T(8,128)(2,1)S(1)} %maximum_bitcast_fusion.18), kind=kOutput, calls=%fused_computation.21 | convolution fusion | flops 2210398208 | bytes 3145728 | tf_op jit(solution)/shard_map/fl,kdlc->kdfc/dot_general | solution.py:86
  652.4 0.0 copy-start
  652.4 64.0 %fusion.24 = f32[2,1,2048,128]{2,3,0,1:T(8,128)S(1)} fusion(bf16[2,2048,128]{1,2,0:T(8,128)(2,1)S(1)} %maximum_bitcast_fusion.20), kind=kOutput, calls=%fused_computation.23 | convolution fusion | flops 2210398208 | bytes 3145728 | tf_op jit(solution)/shard_map/fl,kdlc->kdfc/dot_general | solution.py:87
  716.4 0.0 copy-done
  716.4 0.4 fusion.51
  716.8 0.1 maximum_bitcast_fusion.19
  716.9 0.1 maximum_bitcast_fusion.21
  717.0 63.2 %fusion.21 = f32[2,1,2048,128]{2,3,0,1:T(8,128)S(1)} fusion(bf16[2,2048,128]{1,2,0:T(8,128)(2,1)S(1)} %maximum_bitcast_fusion.19), kind=kOutput, calls=%fused_computation.22 | convolution fusion | flops 2210398208 | bytes 3145728 | tf_op jit(solution)/shard_map/fl,kdfc->kdlc/dot_general | solution.py:94
  780.3 63.5 %fusion.27 = f32[2,1,2048,128]{2,3,0,1:T(8,128)S(1)} fusion(bf16[2,2048,128]{1,2,0:T(8,128)(2,1)S(1)} %maximum_bitcast_fusion.21), kind=kOutput, calls=%fused_computation.24 | convolution fusion | flops 2210398208 | bytes 3145728 | tf_op jit(solution)/shard_map/fl,kdfc->kdlc/dot_general | solution.py:95
  843.8 0.0 copy-start.1
  843.8 0.0 copy-start.2
  843.8 0.4 fusion.56
  844.2 0.8 copy.25
  845.0 0.5 broadcast.173
  845.5 11.7 %reduce.6 = bf16[2048,128]{1,0:T(8,128)(2,1)S(1)} reduce(bf16[2048,1,128]{2,1,0:T(2,128)(2,1)S(1)} %bitcast.126, bf16[]{:T(256)} %broadcast.173), dimensions={1}, to_apply=%bitcast.80.reduce_sub_computation | reduce | bytes 1048578
  857.2 0.9 reshape.172
  858.2 9.5 %all-to-all-start = ((bf16[64,2,2048]{2,1,0:T(2,128)(2,1)}), bf16[64,2,2048]{2,1,0:T(2,128)(2,1)S(1)}, u32[]{:S(2)}, u32[]{:S(2)}) async-start(bf16[64,2,2048]{2,1,0:T(2,128)(2,1)} %reshape.172), calls=%async_computation | async-start | bytes 1048576 | tf_op jit(solution)/shard_map/all_to_all | solution.py:102
  867.7 0.8 copy.26
  868.4 11.5 %reduce.5 = bf16[2048,128]{1,0:T(8,128)(2,1)S(1)} reduce(bf16[2048,1,128]{2,1,0:T(2,128)(2,1)S(1)} %bitcast.127, bf16[]{:T(256)} %broadcast.173), dimensions={1}, to_apply=%bitcast.78.reduce_sub_computation | reduce | bytes 1048578
  880.0 0.9 reshape.170
  880.9 0.0 all-to-all-done
  880.9 9.2 all-to-all-start.1
  890.1 0.7 dynamic-slice_convert_fusion
  890.8 0.0 copy-done.1
  890.8 0.0 copy-done.2
  890.8 0.3 fusion.93
  891.2 0.3 sine_convert_fusion.1
  891.5 0.5 reshape.173
  892.1 8.8 bitcast_reduce_fusion
  900.8 0.2 reshape.163
  901.1 1.7 all-to-all-done.1
  902.7 0.5 reshape.171
  903.3 8.8 bitcast_reduce_fusion.1
  912.0 0.2 reshape.164
  912.3 0.2 add_reduce_fusion
  912.5 1.3 fusion.52
  913.8 0.8 fusion.17
  914.6 2.4 broadcast_multiply_fusion
  (2 shorter events, 0.0 us)
Async XLA Ops:
  6.5 566.4 %all-reduce.4.cloned.1.call-start = ((), (), s32[]{:S(2)}) async-start(), calls=%async_computation.2 | async-start | bytes 2097152 | tf_op jit(solution)/shard_map/psum | solution.py:14
  652.4 64.1 %copy-start = (f32[2048]{0:T(1024)S(1)}, f32[2048]{0:T(1024)}, u32[]{:S(2)}) copy-start(f32[2048]{0:T(1024)} %param.10) | copy-start | bytes 24580
  843.8 47.0 %copy-start.1 = (s32[64]{0:T(128)S(1)}, s32[64]{0:T(128)}, u32[]{:S(2)}) copy-start(s32[64]{0:T(128)} %param.12) | copy-start | bytes 772
  843.8 47.0 %copy-start.2 = (s32[64]{0:T(128)S(1)}, s32[64]{0:T(128)}, u32[]{:S(2)}) copy-start(s32[64]{0:T(128)} %param.11) | copy-start | bytes 772
  858.2 22.7 %all-to-all-start = ((bf16[64,2,2048]{2,1,0:T(2,128)(2,1)}), bf16[64,2,2048]{2,1,0:T(2,128)(2,1)S(1)}, u32[]{:S(2)}, u32[]{:S(2)}) async-start(bf16[64,2,2048]{2,1,0:T(2,128)(2,1)} %reshape.172), calls=%async_computation | async-start | bytes 1048576 | tf_op jit(solution)/shard_map/all_to_all | solution.py:102
  880.9 21.8 %all-to-all-start.1 = ((bf16[64,2,2048]{2,1,0:T(2,128)(2,1)}), bf16[64,2,2048]{2,1,0:T(2,128)(2,1)S(1)}, u32[]{:S(2)}, u32[]{:S(2)}) async-start(bf16[64,2,2048]{2,1,0:T(2,128)(2,1)} %reshape.170), calls=%async_computation.1 | async-start | bytes 1048576 | tf_op jit(solution)/shard_map/all_to_all | solution.py:103
Sparse Core Ops, SparseCore 0:
  10.9 561.9 all-reduce.3
where the time goes:
time: 932 us; the launch traced here: 924 us
  waiting for transfers between devices  563 us (60%)
  matrix products  256 us (27%)
  other arithmetic  35 us (4%)
  local copies, waits for them, and re-layouts  25.4 us (3%)
  starting transfers between devices  18.7 us (2%)
  between operations  16.2 us (2%)
  blocking collectives  10.5 us (1%)
    psum x1, waiting for transfers between devices, broadcast(): return lax.psum(jnp.where(mine, shard, jnp.zeros_like(shard)), axis)  561 us
    dot_general x1, matrix products, shards(): jnp.einsum('fl,kdlc->kdfc', sin_table, pair, preferred_element_type=jnp.f...  64 us
    dot_general x1, matrix products, shards(): jnp.einsum('fl,kdfc->kdlc', sin_table, held, preferred_element_type=jnp.f...  63.5 us
    dot_general x1, matrix products, shards(): jnp.einsum('fl,kdlc->kdfc', cos_table, pair, preferred_element_type=jnp.f...  63.5 us
    dot_general x1, matrix products, shards(): jnp.einsum('fl,kdfc->kdlc', cos_table, held, preferred_element_type=jnp.f...  63.2 us
    unnamed x2, other arithmetic  23.3 us
  transfers between devices with their start and end apart: 3, of which 2 were waited for; matrix products, arithmetic and copies ran while one was open for 3% of the time, Pallas kernels for 0%

commit v1 on v0

--- a/solution.py
+++ b/solution.py
@@ -100,7 +100,10 @@
     lines_dev = lines // date_axis
     my_index = lax.axis_index("date")
     piece_re = lax.all_to_all(filt_re, "date", split_axis=1, concat_axis=0, tiled=True)
-    piece_im = lax.all_to_all(filt_im, "date", split_axis=1, concat_axis=0, tiled=True)
+    piece_im = jnp.concatenate(
+        lax.all_to_all(jnp.stack(jnp.split(filt_im, lax.axis_size("date"), axis=1)), "date", 0, 0),
+        axis=0,
+    )
     row_count = piece_re.shape[1]
     col_count = piece_re.shape[2]
     flat_re = piece_re.reshape(piece_re.shape[0], row_count * col_count)

time: 932 us -> 955 us (1.025)
  local copies, waits for them, and re-layouts: 25.4 us -> 59.3 us
  other arithmetic: 35 us -> 23.6 us
    unnamed x13 -> x75, local copies, waits for them, and re-layouts: 5.92 us -> 42.6 us
    unnamed x2 -> x1, other arithmetic: 23.3 us -> 11.7 us
  transfers between devices with their start and end apart: 3 -> 3, of which waited for: 2 -> 2; matrix products, arithmetic and copies ran while one was open for 3% -> 5% of each run, Pallas kernels for 0% -> 0%
where the time goes in v1:
time: 955 us; the launch traced here: 947 us
  waiting for transfers between devices  563 us (59%)
  matrix products  256 us (27%)
  local copies, waits for them, and re-layouts  59.3 us (6%)
  other arithmetic  23.6 us (2%)
  starting transfers between devices  18.7 us (2%)
  between operations  16.2 us (2%)
  blocking collectives  10.5 us (1%)
    psum x1, waiting for transfers between devices, broadcast(): return lax.psum(jnp.where(mine, shard, jnp.zeros_like(shard)), axis)  561 us
    dot_general x1, matrix products, shards(): jnp.einsum('fl,kdlc->kdfc', sin_table, pair, preferred_element_type=jnp.f...  64.1 us
    dot_general x1, matrix products, shards(): jnp.einsum('fl,kdfc->kdlc', sin_table, held, preferred_element_type=jnp.f...  63.5 us
    dot_general x1, matrix products, shards(): jnp.einsum('fl,kdlc->kdfc', cos_table, pair, preferred_element_type=jnp.f...  63.5 us
    dot_general x1, matrix products, shards(): jnp.einsum('fl,kdfc->kdlc', cos_table, held, preferred_element_type=jnp.f...  63.2 us
    unnamed x75, local copies, waits for them, and re-layouts  42.6 us
  transfers between devices with their start and end apart: 3, of which 2 were waited for; matrix products, arithmetic and copies ran while one was open for 5% of the time, Pallas kernels for 0%

profile of v1, /device:TPU:1, one launch (start us, length us, event | category | flops | bytes accessed | tf_op | source)
XLA Modules:
  0.0 946.7 jit_solution(3790334989144324326)
XLA Ops:
  6.5 1.2 copy.20
  7.8 1.2 copy.21
  9.7 1.0 select_bitcast_fusion
  10.8 0.9 fusion.39
  11.7 561.2 %all-reduce.4.cloned.1.call-done = (bf16[2048,128]{0,1:T(8,128)(2,1)}, bf16[2048,128]{0,1:T(8,128)(2,1)}) async-done(((bf16[2048,128]{0,1:T(8,128)(2,1)}, bf16[2048,128]{0,1:T(8,128)(2,1)}), (bf16[2048,128]{0,1:T(8,128)(2,1)}, bf16[2048,128]{0,1:T(8,128)(2,1)})) %all-reduce.4.cloned.1.call-update) | async-done | bytes 1048592 | tf_op jit(solution)/shard_map/psum | solution.py:14
  572.9 2.1 fusion.41
  575.0 10.5 %all-reduce = (f32[]{:T(128)}, f32[1]{0:T(128)}) all-reduce(f32[]{:T(128)} %fusion.41, f32[1]{0:T(128)} %bitcast), channel_id=1, replica_groups=mesh['date'=64,'rng'=4] {'rng'}, use_global_device_ids=true, to_apply=%region_5.6 | all-reduce | flops 2 | bytes 16 | tf_op jit(solution)/shard_map/psum | solution.py:75
  586.9 1.7 fusion.59
  588.8 63.5 %fusion.18 = f32[2,1,2048,128]{2,3,0,1:T(8,128)S(1)} fusion(bf16[2,2048,128]{1,2,0:T(8,128)(2,1)S(1)} %maximum_bitcast_fusion.18), kind=kOutput, calls=%fused_computation.21 | convolution fusion | flops 2210398208 | bytes 3145728 | tf_op jit(solution)/shard_map/fl,kdlc->kdfc/dot_general | solution.py:86
  652.3 64.1 %fusion.24 = f32[2,1,2048,128]{2,3,0,1:T(8,128)S(1)} fusion(bf16[2,2048,128]{1,2,0:T(8,128)(2,1)S(1)} %maximum_bitcast_fusion.20), kind=kOutput, calls=%fused_computation.23 | convolution fusion | flops 2210398208 | bytes 3145728 | tf_op jit(solution)/shard_map/fl,kdlc->kdfc/dot_general | solution.py:87
  717.0 63.2 %fusion.21 = f32[2,1,2048,128]{2,3,0,1:T(8,128)S(1)} fusion(bf16[2,2048,128]{1,2,0:T(8,128)(2,1)S(1)} %maximum_bitcast_fusion.19), kind=kOutput, calls=%fused_computation.22 | convolution fusion | flops 2210398208 | bytes 3145728 | tf_op jit(solution)/shard_map/fl,kdfc->kdlc/dot_general | solution.py:94
  780.2 63.5 %fusion.27 = f32[2,1,2048,128]{2,3,0,1:T(8,128)S(1)} fusion(bf16[2,2048,128]{1,2,0:T(8,128)(2,1)S(1)} %maximum_bitcast_fusion.21), kind=kOutput, calls=%fused_computation.24 | convolution fusion | flops 2210398208 | bytes 3145728 | tf_op jit(solution)/shard_map/fl,kdfc->kdlc/dot_general | solution.py:95
  845.0 0.6 constant_dynamic-update-slice_fusion.63
  850.5 0.8 copy.25
  851.8 11.7 %reduce.3 = bf16[2048,128]{1,0:T(8,128)(2,1)S(1)} reduce(bf16[2048,1,128]{2,1,0:T(2,128)(2,1)S(1)} %bitcast.260, bf16[]{:T(256)} %broadcast.172), dimensions={1}, to_apply=%bitcast.212.reduce_sub_computation | reduce | bytes 1048578
  863.6 0.9 reshape.165
  864.5 9.5 %all-to-all-start = ((bf16[64,2,2048]{2,1,0:T(2,128)(2,1)}), bf16[64,2,2048]{2,1,0:T(2,128)(2,1)S(1)}, u32[]{:S(2)}, u32[]{:S(2)}) async-start(bf16[64,2,2048]{2,1,0:T(2,128)(2,1)} %reshape.165), calls=%async_computation | async-start | bytes 1048576 | tf_op jit(solution)/shard_map/all_to_all | solution.py:102
  874.0 0.6 constant_dynamic-update-slice_fusion.62
  874.6 0.6 constant_dynamic-update-slice_fusion.61
  875.2 0.6 constant_dynamic-update-slice_fusion.60
  875.8 0.6 constant_dynamic-update-slice_fusion.59
  876.4 0.6 constant_dynamic-update-slice_fusion.58
  877.0 0.6 constant_dynamic-update-slice_fusion.57
  877.6 0.6 constant_dynamic-update-slice_fusion.56
  878.2 0.6 constant_dynamic-update-slice_fusion.55
  878.8 0.6 constant_dynamic-update-slice_fusion.54
  879.4 0.6 constant_dynamic-update-slice_fusion.53
  880.0 0.6 constant_dynamic-update-slice_fusion.52
  880.6 0.6 constant_dynamic-update-slice_fusion.51
  881.2 0.6 constant_dynamic-update-slice_fusion.50
  881.8 0.6 constant_dynamic-update-slice_fusion.49
  882.4 0.6 constant_dynamic-update-slice_fusion.48
  883.0 0.6 constant_dynamic-update-slice_fusion.47
  883.6 0.6 constant_dynamic-update-slice_fusion.46
  884.2 0.6 constant_dynamic-update-slice_fusion.45
  884.8 0.6 constant_dynamic-update-slice_fusion.44
  885.4 0.6 constant_dynamic-update-slice_fusion.43
  886.0 0.6 constant_dynamic-update-slice_fusion.42
  886.6 0.6 constant_dynamic-update-slice_fusion.41
  887.2 0.6 constant_dynamic-update-slice_fusion.40
  887.8 0.6 constant_dynamic-update-slice_fusion.39
  888.4 0.6 constant_dynamic-update-slice_fusion.38
  889.0 0.6 constant_dynamic-update-slice_fusion.37
  889.6 0.6 constant_dynamic-update-slice_fusion.36
  890.2 0.6 constant_dynamic-update-slice_fusion.35
  892.0 0.6 constant_dynamic-update-slice_fusion.32
  893.8 0.6 constant_dynamic-update-slice_fusion.29
  895.5 0.6 constant_dynamic-update-slice_fusion.26
  897.3 0.6 constant_dynamic-update-slice_fusion.23
  899.1 0.6 constant_dynamic-update-slice_fusion.20
  900.9 0.6 constant_dynamic-update-slice_fusion.17
  901.5 0.6 constant_dynamic-update-slice_fusion.16
  903.3 0.6 constant_dynamic-update-slice_fusion.13
  905.1 0.6 constant_dynamic-update-slice_fusion.10
  907.1 0.6 constant_dynamic-update-slice_fusion.8
  909.0 0.6 constant_dynamic-update-slice_fusion.5
  910.8 0.6 constant_dynamic-update-slice_fusion.2
  912.6 9.2 all-to-all-start.1
  921.8 0.7 dynamic-slice_convert_fusion
  923.7 8.8 bitcast_reduce_fusion
  932.7 1.7 all-to-all-done.1
  935.0 1.3 fusion.52
  936.2 0.8 fusion.17
  937.0 2.4 broadcast_multiply_fusion
  (115 shorter events, 24.0 us)
Async XLA Ops:
  6.5 566.4 %all-reduce.4.cloned.1.call-start = ((), (), s32[]{:S(2)}) async-start(), calls=%async_computation.2 | async-start | bytes 2097152 | tf_op jit(solution)/shard_map/psum | solution.py:14
  652.3 64.1 %copy-start = (f32[2048]{0:T(1024)S(1)}, f32[2048]{0:T(1024)}, u32[]{:S(2)}) copy-start(f32[2048]{0:T(1024)} %param.10) | copy-start | bytes 24580
  844.1 78.4 %copy-start.1 = (s32[64]{0:T(128)S(1)}, s32[64]{0:T(128)}, u32[]{:S(2)}) copy-start(s32[64]{0:T(128)} %param.12) | copy-start | bytes 772
  844.1 78.4 %copy-start.2 = (s32[64]{0:T(128)S(1)}, s32[64]{0:T(128)}, u32[]{:S(2)}) copy-start(s32[64]{0:T(128)} %param.11) | copy-start | bytes 772
  864.5 48.1 %all-to-all-start = ((bf16[64,2,2048]{2,1,0:T(2,128)(2,1)}), bf16[64,2,2048]{2,1,0:T(2,128)(2,1)S(1)}, u32[]{:S(2)}, u32[]{:S(2)}) async-start(bf16[64,2,2048]{2,1,0:T(2,128)(2,1)} %reshape.165), calls=%async_computation | async-start | bytes 1048576 | tf_op jit(solution)/shard_map/all_to_all | solution.py:102
  912.6 21.8 %all-to-all-start.1 = ((bf16[64,1,32,128]{3,2,1,0:T(8,128)(2,1)}), bf16[64,1,32,128]{3,2,1,0:T(8,128)(2,1)S(1)}, u32[]{:S(2)}, u32[]{:S(2)}) async-start(bf16[64,1,32,128]{3,2,1,0:T(8,128)(2,1)} %constant_dynamic-update-slice_fusion), calls=%async_computation.1 | async-start | bytes 1048576 | tf_op jit(solution)/shard_map/all_to_all | solution.py:104
Sparse Core Ops, SparseCore 0:
  10.9 561.9 all-reduce.3
